TPU v7x, 32 devices: a whole 2x2x4 slice. The times are simulated.
32 devices in a mesh: groups: 2 (over y), cam: 4 (over z), tm: 2 (over x), chan: 2 (over core).
Axes of the slice: x: 2, y: 2, z: 4, core: 2. Of those that a mesh axis runs over, the one named last changes fastest.
Arguments:
- video: bfloat16 [16, 8, 16, 8, 256], P(('groups', 'cam'), 'tm', None, None, 'chan'), parts along dimension 0, may hold values from -6 to 6
- conv_weight: bfloat16 [27, 256, 256], P(None, None, 'chan'), may hold values from -0.078125 to 0.078125
- proj_weight: bfloat16 [256, 16], P('chan'), may hold values from -0.375 to 0.375
- rig_sizes: int32 [8], P('groups'), parts along dimension 0, may hold values from 1 to 3, as said below
- camera_order: int32 [16], P('groups'), parts along dimension 0, may hold values from 0 to 7, as said below
- owner_slot: int32 [8], P('groups'), parts along dimension 0, may hold values from 0 to 3, as said below
- cotangent: bfloat16 [8, 8, 16, 128], P(('groups', 'cam'), 'tm'), parts along dimension 0, may hold values from -6 to 6
Outputs:
- robot_latent: float32 [8, 8, 16, 128], P(('groups', 'cam'), 'tm'), parts along dimension 0
- grad_conv: bfloat16 [54, 256, 256], P('groups', None, 'chan'), parts along dimension 0
- grad_proj: float32 [512, 16], P(('groups', 'chan')), parts along dimension 0
- grad_video: bfloat16 [16, 8, 16, 8, 256], P(('groups', 'cam'), 'tm', None, None, 'chan'), parts along dimension 0
There are 2 independent parts, one for each index of `groups`. A program takes and returns all parts, laid end to end along the dimension named above; an argument that names none is the same for every part. Nothing has to cross between parts.
Inputs may be any that keep to these rules, and one draw needn't show every extreme that they name: `rig_sizes`: the sizes sum to 8; the largest is exactly 3. `camera_order`: A permutation; the cameras whose places fall from rig_sizes[0] + ... + rig_sizes[r-1] to below rig_sizes[0] + ... + rig_sizes[r] belong to robot r. `owner_slot`: A permutation of the output rows.
All inputs are finite; a program needn't handle non-finite values.
Results may differ from a plain program's by a relative error of at most 0.0059.
Values may be sent and summed in bfloat16 or wider, within the bound.
No kernel may reach another device: no remote copies, remote signals or barrier semaphores. Data moves between devices by JAX's collectives and lax.ppermute only.
A program may use at most 128 MiB of HBM per device.

v0:
```python
import jax
import jax.numpy as jnp
from jax import lax
from jax.sharding import PartitionSpec as P

KT = 3
KS = 3


def shifted(shard, axis, by):
    size = lax.axis_size(axis)
    pairs = [(i, i + by) for i in range(size) if 0 <= i + by < size]
    return lax.ppermute(shard, axis, pairs)


def tap_offsets():
    return [
        (shift_t, shift_h, shift_w)
        for shift_t in range(KT)
        for shift_h in range(KS)
        for shift_w in range(KS)
    ]


def forward_taps(extended, weight, frames, height, width):
    channels = extended.shape[-1]
    summed = jnp.zeros((extended.shape[0] * frames * height * width, weight.shape[2]), jnp.float32)
    for tap_index, (shift_t, shift_h, shift_w) in enumerate(tap_offsets()):
        window = extended[
            :, shift_t : shift_t + frames, shift_h : shift_h + height, shift_w : shift_w + width, :
        ].reshape(-1, channels)
        summed = summed + jnp.dot(window, weight[tap_index], preferred_element_type=jnp.float32)
    return summed


def weight_taps(extended, grad_rows, frames, height, width):
    channels = extended.shape[-1]
    results = []
    for shift_t, shift_h, shift_w in tap_offsets():
        window = extended[
            :, shift_t : shift_t + frames, shift_h : shift_h + height, shift_w : shift_w + width, :
        ].reshape(-1, channels)
        results.append(
            lax.dot_general(
                window, grad_rows, (((0,), (0,)), ((), ())), preferred_element_type=jnp.float32
            )
        )
    return jnp.stack(results)


def input_taps(grad_rows, weight, batch, frames, height, width):
    channels = weight.shape[1]
    pad_half = KS // 2
    padded = jnp.zeros(
        (batch, frames + KT - 1, height + KS - 1, width + KS - 1, channels), jnp.float32
    )
    for tap_index, (shift_t, shift_h, shift_w) in enumerate(tap_offsets()):
        backed = lax.dot_general(
            grad_rows,
            weight[tap_index],
            (((1,), (1,)), ((), ())),
            preferred_element_type=jnp.float32,
        )
        padded = padded.at[
            :, shift_t : shift_t + frames, shift_h : shift_h + height, shift_w : shift_w + width, :
        ].add(backed.reshape(batch, frames, height, width, channels))
    return padded[:, :, pad_half : pad_half + height, pad_half : pad_half + width, :]


def joining_matrix(rig_sizes, camera_order, owner_slot):
    robots = rig_sizes.shape[0]
    ends = jnp.cumsum(rig_sizes)
    robot_of = jnp.sum((ends[None, :] <= camera_order[:, None]).astype(jnp.int32), axis=1)
    member = robot_of[:, None] == jnp.arange(robots, dtype=jnp.int32)[None, :]
    slot_of = jnp.sum(jnp.where(member, owner_slot[None, :], 0), axis=1)
    count_of = jnp.sum(jnp.where(member, rig_sizes[None, :], 0), axis=1)
    share = 1.0 / count_of.astype(jnp.float32)
    placed = slot_of[None, :] == jnp.arange(robots, dtype=jnp.int32)[:, None]
    return jnp.where(placed, share[None, :], jnp.zeros_like(share)[None, :])


def body(video, conv_weight, proj_weight, rig_sizes, camera_order, owner_slot, cotangent):
    cam_dev, frames, height, width, half_chan = video.shape
    pad_half = KS // 2
    lat_width = proj_weight.shape[1]
    cache_half = shifted(video[:, frames - (KT - 1) :], "tm", 1)
    whole_now, whole_cache = (
        lax.all_gather(video, "chan", axis=4, tiled=True),
        lax.all_gather(cache_half, "chan", axis=4, tiled=True),
    )
    extended = jnp.concatenate([whole_cache, whole_now], axis=1)
    extended = jnp.pad(
        extended, ((0, 0), (0, 0), (pad_half, pad_half), (pad_half, pad_half), (0, 0))
    )
    pre = forward_taps(extended, conv_weight, frames, height, width)
    sigma = jax.nn.sigmoid(pre)
    act = (pre * sigma).astype(jnp.bfloat16)
    latent_part = jnp.dot(act, proj_weight, preferred_element_type=jnp.float32)
    latent = lax.psum(latent_part, "chan").astype(jnp.bfloat16)
    mixing = joining_matrix(rig_sizes, camera_order, owner_slot)
    cam_index = lax.axis_index("cam")
    my_row = lax.dynamic_slice_in_dim(mixing, cam_index, 1, 0)
    latent_maps = latent.reshape(cam_dev, frames, height, width * lat_width)
    block_in = lax.all_gather(latent_maps, "cam", axis=0, tiled=True)
    count_in = block_in.shape[0]
    flat_in = block_in.reshape(count_in, -1).astype(jnp.float32)
    added = jnp.dot(
        my_row, flat_in, precision=lax.Precision.HIGHEST, preferred_element_type=jnp.float32
    )
    robot_latent = added.reshape(
        jnp.zeros((1, frames, height, width * lat_width), jnp.float32).shape
    )
    my_cols = lax.dynamic_slice_in_dim(mixing, cam_index * cam_dev, cam_dev, 1)
    block_in = lax.all_gather(cotangent, "cam", axis=0, tiled=True)
    count_in = block_in.shape[0]
    flat_in = block_in.reshape(count_in, -1).astype(jnp.float32)
    spread = lax.dot_general(
        my_cols,
        flat_in,
        (((0,), (0,)), ((), ())),
        precision=lax.Precision.HIGHEST,
        preferred_element_type=jnp.float32,
    )
    dlatent = spread.astype(jnp.bfloat16).reshape(-1, lat_width)
    grad_proj_local = lax.dot_general(
        act, dlatent, (((0,), (0,)), ((), ())), preferred_element_type=jnp.float32
    )
    dact = lax.dot_general(
        dlatent, proj_weight, (((1,), (1,)), ((), ())), preferred_element_type=jnp.float32
    )
    dpre = (dact * sigma * (1.0 + pre * (1.0 - sigma))).astype(jnp.bfloat16)
    full_back = input_taps(dpre, conv_weight, cam_dev, frames, height, width)
    cache_part = full_back[:, : KT - 1]
    incoming = shifted(cache_part, "tm", -1)
    own_part = full_back[:, KT - 1 :]
    own_part = own_part.at[:, frames - (KT - 1) :].add(incoming)
    grad_conv_local = weight_taps(extended, dpre, frames, height, width)
    grad_conv, grad_proj = lax.psum((grad_conv_local, grad_proj_local), ("cam", "tm"))
    grad_video = lax.psum_scatter(
        own_part.astype(jnp.bfloat16), "chan", scatter_dimension=4, tiled=True
    )
    return (robot_latent, grad_conv.astype(jnp.bfloat16), grad_proj, grad_video)


def solution(mesh):
    return jax.shard_map(
        body,
        mesh=mesh,
        in_specs=(
            P(("groups", "cam"), "tm", None, None, "chan"),
            P(None, None, "chan"),
            P("chan", None),
            P("groups"),
            P("groups"),
            P("groups"),
            P(("groups", "cam"), "tm", None, None),
        ),
        out_specs=(
            P(("groups", "cam"), "tm", None, None),
            P("groups", None, "chan"),
            P(("groups", "chan"), None),
            P(("groups", "cam"), "tm", None, None, "chan"),
        ),
        check_vma=False,
    )
```

profile of v0, /device:TPU:0, one launch (start us, length us, event | category | flops | bytes accessed | tf_op | source)
XLA Modules:
  0.0 450.1 jit_solution(12302339504369722204)
XLA Ops:
  8.2 4.8 %collective-permute-start = (bf16[2,2,16,8,128]{4,3,2,1,0:T(8,128)(2,1)S(1)}, bf16[2,2,16,8,128]{4,3,2,1,0:T(8,128)(2,1)S(1)}, u32[]{:S(2)}, u32[]{:S(2)}) collective-permute-start(bf16[2,2,16,8,128]{4,3,2,1,0:T(8,128)(2,1)S(1)} %slice.1486), channel_id=1, source_target_pairs={{0,2},{1,3},{4,6},{5,7},{8,10},{9,11},{12,14},{13,15},{16,18},{17,... | collective-permute-start | bytes 393224 | tf_op jit(solution)/shard_map/ppermute | solution.py:13
  15.4 13.6 %all_gather.15 = bf16[4,4,16,128]{3,2,1,0:T(8,128)(2,1)S(1)} all-gather(bf16[1,4,16,128]{3,2,1,0:T(8,128)(2,1)} %param.69), channel_id=1, replica_groups=mesh['groups'=2,'cam'=4,'tm'=2,'chan'=2] {'cam'}, dimensions={0}, use_global_device_ids=true | all-gather | bytes 81920 | tf_op jit(solution)/shard_map/all_gather | solution.py:114
  30.2 2.4 all_gather.13
  32.5 2.0 all_gather.12
  35.0 2.3 pad_slice_fusion
  58.1 2.2 scatter-add.94
  60.3 6.7 %scatter-add.95 = f32[2,6,18,10,256]{4,3,2,1,0:T(8,128)} dynamic-update-slice(f32[2,6,18,10,256]{4,3,2,1,0:T(8,128)} %scatter-add.94, f32[2,4,16,8,256]{4,3,2,1,0:T(8,128)S(1)} %convolution_add_fusion.25, s32[]{:T(128)} %constant.917.clone.1, s32[]{:T(128)} %constant.917.clone.1, s32[]{:T(128)} %constant.917.clone.1, s32[]{:T(128)} %constant.926.clone.1, s32[]{:T(128)} %constant.917.clone.1) | dynamic-update-slice | bytes 2097156 | tf_op jit(solution)/shard_map/scatter-add | solution.py:66
  68.9 6.7 %scatter-add.96 = f32[2,6,18,10,256]{4,3,2,1,0:T(8,128)} dynamic-update-slice(f32[2,6,18,10,256]{4,3,2,1,0:T(8,128)} %scatter-add.95, f32[2,4,16,8,256]{4,3,2,1,0:T(8,128)S(1)} %convolution_add_fusion.24, s32[]{:T(128)} %constant.917.clone.1, s32[]{:T(128)} %constant.917.clone.1, s32[]{:T(128)} %constant.917.clone.1, s32[]{:T(128)} %constant.924.clone.1, s32[]{:T(128)} %constant.917.clone.1) | dynamic-update-slice | bytes 2097156 | tf_op jit(solution)/shard_map/scatter-add | solution.py:66
  75.6 2.6 fusion.7
  80.0 6.7 %scatter-add.100 = f32[2,6,18,10,256]{4,3,2,1,0:T(8,128)} dynamic-update-slice(f32[2,6,18,10,256]{4,3,2,1,0:T(8,128)} %fusion.7, f32[2,4,16,8,256]{4,3,2,1,0:T(8,128)S(1)} %convolution_add_fusion.22, s32[]{:T(128)} %constant.917.clone.1, s32[]{:T(128)} %constant.917.clone.1, s32[]{:T(128)} %constant.926.clone.1, s32[]{:T(128)} %constant.926.clone.1, s32[]{:T(128)} %constant.917.clone.1) | dynamic-update-slice | bytes 2097156 | tf_op jit(solution)/shard_map/scatter-add | solution.py:66
  86.7 3.8 convolution_add_fusion.21
  90.5 8.6 %scatter-add.101 = f32[2,6,18,10,256]{4,3,2,1,0:T(8,128)} dynamic-update-slice(f32[2,6,18,10,256]{4,3,2,1,0:T(8,128)} %scatter-add.100, f32[2,4,16,8,256]{4,3,2,1,0:T(8,128)S(1)} %convolution_add_fusion.21, s32[]{:T(128)} %constant.917.clone.1, s32[]{:T(128)} %bitcast.103, s32[]{:T(128)} %bitcast.104, s32[]{:T(128)} %bitcast.105, s32[]{:T(128)} %constant.917.clone.1) | dynamic-update-slice | bytes 2097156 | tf_op jit(solution)/shard_map/scatter-add | solution.py:66
  99.1 2.6 fusion.6
  101.8 1.9 convolution_add_fusion.19
  103.6 6.7 %scatter-add.105 = f32[2,6,18,10,256]{4,3,2,1,0:T(8,128)} dynamic-update-slice(f32[2,6,18,10,256]{4,3,2,1,0:T(8,128)} %fusion.6, f32[2,4,16,8,256]{4,3,2,1,0:T(8,128)S(1)} %convolution_add_fusion.19, s32[]{:T(128)} %constant.917.clone.1, s32[]{:T(128)} %constant.917.clone.1, s32[]{:T(128)} %constant.924.clone.1, s32[]{:T(128)} %constant.926.clone.1, s32[]{:T(128)} %constant.917.clone.1) | dynamic-update-slice | bytes 2097156 | tf_op jit(solution)/shard_map/scatter-add | solution.py:66
  110.3 1.9 convolution_add_fusion.18
  112.2 6.7 %scatter-add.106 = f32[2,6,18,10,256]{4,3,2,1,0:T(8,128)} dynamic-update-slice(f32[2,6,18,10,256]{4,3,2,1,0:T(8,128)} %scatter-add.105, f32[2,4,16,8,256]{4,3,2,1,0:T(8,128)S(1)} %convolution_add_fusion.18, s32[]{:T(128)} %constant.917.clone.1, s32[]{:T(128)} %constant.917.clone.1, s32[]{:T(128)} %constant.924.clone.1, s32[]{:T(128)} %constant.924.clone.1, s32[]{:T(128)} %constant.917.clone.1) | dynamic-update-slice | bytes 2097156 | tf_op jit(solution)/shard_map/scatter-add | solution.py:66
  118.9 2.7 fusion.5
  121.6 1.9 convolution_add_fusion.16
  123.4 6.8 %scatter-add.110 = f32[2,6,18,10,256]{4,3,2,1,0:T(8,128)} dynamic-update-slice(f32[2,6,18,10,256]{4,3,2,1,0:T(8,128)} %fusion.5, f32[2,4,16,8,256]{4,3,2,1,0:T(8,128)S(1)} %convolution_add_fusion.16, s32[]{:T(128)} %constant.917.clone.1, s32[]{:T(128)} %constant.926.clone.1, s32[]{:T(128)} %constant.917.clone.1, s32[]{:T(128)} %constant.926.clone.1, s32[]{:T(128)} %constant.917.clone.1) | dynamic-update-slice | bytes 2097156 | tf_op jit(solution)/shard_map/scatter-add | solution.py:66
  130.2 1.9 convolution_add_fusion.15
  132.1 6.8 %scatter-add.111 = f32[2,6,18,10,256]{4,3,2,1,0:T(8,128)} dynamic-update-slice(f32[2,6,18,10,256]{4,3,2,1,0:T(8,128)} %scatter-add.110, f32[2,4,16,8,256]{4,3,2,1,0:T(8,128)S(1)} %convolution_add_fusion.15, s32[]{:T(128)} %constant.917.clone.1, s32[]{:T(128)} %constant.926.clone.1, s32[]{:T(128)} %constant.917.clone.1, s32[]{:T(128)} %constant.924.clone.1, s32[]{:T(128)} %constant.917.clone.1) | dynamic-update-slice | bytes 2097156 | tf_op jit(solution)/shard_map/scatter-add | solution.py:66
  138.9 2.7 fusion.4
  141.5 1.9 convolution_add_fusion.13
  143.4 6.7 %scatter-add.115 = f32[2,6,18,10,256]{4,3,2,1,0:T(8,128)} dynamic-update-slice(f32[2,6,18,10,256]{4,3,2,1,0:T(8,128)} %fusion.4, f32[2,4,16,8,256]{4,3,2,1,0:T(8,128)S(1)} %convolution_add_fusion.13, s32[]{:T(128)} %constant.917.clone.1, s32[]{:T(128)} %constant.926.clone.1, s32[]{:T(128)} %constant.926.clone.1, s32[]{:T(128)} %constant.926.clone.1, s32[]{:T(128)} %constant.917.clone.1) | dynamic-update-slice | bytes 2097156 | tf_op jit(solution)/shard_map/scatter-add | solution.py:66
  152.0 6.7 %scatter-add.116 = f32[2,6,18,10,256]{4,3,2,1,0:T(8,128)} dynamic-update-slice(f32[2,6,18,10,256]{4,3,2,1,0:T(8,128)} %scatter-add.115, f32[2,4,16,8,256]{4,3,2,1,0:T(8,128)S(1)} %convolution_add_fusion.12, s32[]{:T(128)} %constant.917.clone.1, s32[]{:T(128)} %constant.926.clone.1, s32[]{:T(128)} %constant.926.clone.1, s32[]{:T(128)} %constant.924.clone.1, s32[]{:T(128)} %constant.917.clone.1) | dynamic-update-slice | bytes 2097156 | tf_op jit(solution)/shard_map/scatter-add | solution.py:66
  158.8 2.7 fusion.3
  161.4 1.9 convolution_add_fusion.10
  163.3 6.7 %scatter-add.120 = f32[2,6,18,10,256]{4,3,2,1,0:T(8,128)} dynamic-update-slice(f32[2,6,18,10,256]{4,3,2,1,0:T(8,128)} %fusion.3, f32[2,4,16,8,256]{4,3,2,1,0:T(8,128)S(1)} %convolution_add_fusion.10, s32[]{:T(128)} %constant.917.clone.1, s32[]{:T(128)} %constant.926.clone.1, s32[]{:T(128)} %constant.924.clone.1, s32[]{:T(128)} %constant.926.clone.1, s32[]{:T(128)} %constant.917.clone.1) | dynamic-update-slice | bytes 2097156 | tf_op jit(solution)/shard_map/scatter-add | solution.py:66
  170.1 1.9 convolution_add_fusion.9
  172.0 6.7 %scatter-add.121 = f32[2,6,18,10,256]{4,3,2,1,0:T(8,128)} dynamic-update-slice(f32[2,6,18,10,256]{4,3,2,1,0:T(8,128)} %scatter-add.120, f32[2,4,16,8,256]{4,3,2,1,0:T(8,128)S(1)} %convolution_add_fusion.9, s32[]{:T(128)} %constant.917.clone.1, s32[]{:T(128)} %constant.926.clone.1, s32[]{:T(128)} %constant.924.clone.1, s32[]{:T(128)} %constant.924.clone.1, s32[]{:T(128)} %constant.917.clone.1) | dynamic-update-slice | bytes 2097156 | tf_op jit(solution)/shard_map/scatter-add | solution.py:66
  178.7 2.6 fusion.2
  183.2 6.7 %scatter-add.125 = f32[2,6,18,10,256]{4,3,2,1,0:T(8,128)} dynamic-update-slice(f32[2,6,18,10,256]{4,3,2,1,0:T(8,128)} %fusion.2, f32[2,4,16,8,256]{4,3,2,1,0:T(8,128)S(1)} %convolution_add_fusion.7, s32[]{:T(128)} %constant.917.clone.1, s32[]{:T(128)} %constant.924.clone.1, s32[]{:T(128)} %constant.917.clone.1, s32[]{:T(128)} %constant.926.clone.1, s32[]{:T(128)} %constant.917.clone.1) | dynamic-update-slice | bytes 2097156 | tf_op jit(solution)/shard_map/scatter-add | solution.py:66
  191.8 6.7 %scatter-add.126 = f32[2,6,18,10,256]{4,3,2,1,0:T(8,128)} dynamic-update-slice(f32[2,6,18,10,256]{4,3,2,1,0:T(8,128)} %scatter-add.125, f32[2,4,16,8,256]{4,3,2,1,0:T(8,128)S(1)} %convolution_add_fusion.6, s32[]{:T(128)} %constant.917.clone.1, s32[]{:T(128)} %constant.924.clone.1, s32[]{:T(128)} %constant.917.clone.1, s32[]{:T(128)} %constant.924.clone.1, s32[]{:T(128)} %constant.917.clone.1) | dynamic-update-slice | bytes 2097156 | tf_op jit(solution)/shard_map/scatter-add | solution.py:66
  198.5 2.6 fusion.1
  203.0 7.0 %scatter-add.130 = f32[2,6,18,10,256]{4,3,2,1,0:T(8,128)} dynamic-update-slice(f32[2,6,18,10,256]{4,3,2,1,0:T(8,128)} %fusion.1, f32[2,4,16,8,256]{4,3,2,1,0:T(8,128)S(1)} %convolution_add_fusion.4, s32[]{:T(128)} %constant.917.clone.1, s32[]{:T(128)} %constant.924.clone.1, s32[]{:T(128)} %constant.926.clone.1, s32[]{:T(128)} %constant.926.clone.1, s32[]{:T(128)} %constant.917.clone.1) | dynamic-update-slice | bytes 2097156 | tf_op jit(solution)/shard_map/scatter-add | solution.py:66
  211.9 6.7 %scatter-add.131 = f32[2,6,18,10,256]{4,3,2,1,0:T(8,128)} dynamic-update-slice(f32[2,6,18,10,256]{4,3,2,1,0:T(8,128)} %scatter-add.130, f32[2,4,16,8,256]{4,3,2,1,0:T(8,128)S(1)} %convolution_add_fusion.3, s32[]{:T(128)} %constant.917.clone.1, s32[]{:T(128)} %constant.924.clone.1, s32[]{:T(128)} %constant.926.clone.1, s32[]{:T(128)} %constant.924.clone.1, s32[]{:T(128)} %constant.917.clone.1) | dynamic-update-slice | bytes 2097156 | tf_op jit(solution)/shard_map/scatter-add | solution.py:66
  218.6 2.6 fusion
  223.1 6.7 %scatter-add.135 = f32[2,6,18,10,256]{4,3,2,1,0:T(8,128)} dynamic-update-slice(f32[2,6,18,10,256]{4,3,2,1,0:T(8,128)} %fusion, f32[2,4,16,8,256]{4,3,2,1,0:T(8,128)S(1)} %convolution_add_fusion.1, s32[]{:T(128)} %constant.917.clone.1, s32[]{:T(128)} %constant.924.clone.1, s32[]{:T(128)} %constant.924.clone.1, s32[]{:T(128)} %constant.926.clone.1, s32[]{:T(128)} %constant.917.clone.1) | dynamic-update-slice | bytes 2097156 | tf_op jit(solution)/shard_map/scatter-add | solution.py:66
  229.8 1.9 convolution_add_fusion
  231.7 6.7 %scatter-add.136 = f32[2,6,18,10,256]{4,3,2,1,0:T(8,128)} dynamic-update-slice(f32[2,6,18,10,256]{4,3,2,1,0:T(8,128)} %scatter-add.135, f32[2,4,16,8,256]{4,3,2,1,0:T(8,128)S(1)} %convolution_add_fusion, s32[]{:T(128)} %constant.917.clone.1, s32[]{:T(128)} %constant.924.clone.1, s32[]{:T(128)} %constant.924.clone.1, s32[]{:T(128)} %constant.924.clone.1, s32[]{:T(128)} %constant.917.clone.1) | dynamic-update-slice | bytes 2097156 | tf_op jit(solution)/shard_map/scatter-add | solution.py:66
  240.9 3.6 psum.21
  246.6 13.4 %all_gather.14 = bf16[8,4,16,128]{3,2,1,0:T(8,128)(2,1)S(1)} all-gather(bf16[2,4,16,128]{3,2,1,0:T(8,128)(2,1)S(1)} %reshape.1490), channel_id=1, replica_groups=mesh['groups'=2,'cam'=4,'tm'=2,'chan'=2] {'cam'}, dimensions={0}, use_global_device_ids=true | all-gather | bytes 163840 | tf_op jit(solution)/shard_map/all_gather | solution.py:104
  262.5 11.8 %copy.48 = bf16[2,4,16,8,256]{3,2,1,0,4:T(8,128)(2,1)} copy(bf16[2,4,16,8,256]{4,3,2,1,0:T(8,128)(2,1)S(1)} %fusion.37) | data formatting | bytes 1048576
  274.3 13.6 %reshape.1527 = bf16[256,1024]{1,0:T(8,128)(2,1)} reshape(bf16[256,2,4,16,8]{4,3,2,1,0:T(8,128)(2,1)} %bitcast.557) | data formatting | bytes 1048576
  288.0 142.3 %all-reduce.4 = (bf16[27,256,128]{2,1,0:T(8,128)(2,1)}, f32[128,16]{0,1:T(8,128)}) all-reduce(f32[27,256,128]{2,1,0:T(8,128)S(1)} %copy-done.4, f32[128,16]{0,1:T(8,128)S(1)} %fusion.156), channel_id=1, replica_groups=mesh['groups'=2,'cam'=4,'tm'=2,'chan'=2] {'cam','tm'}, use_global_device_ids=true, to_apply=%region_5.6 | all-reduce | flops 886784 | bytes 5324800 | tf_op jit(solution)/shard_map/psum | solution.py:138
  430.3 6.8 %reshape.1528 = bf16[128,2,4,16,8]{4,3,2,1,0:T(8,128)(2,1)} reshape(bf16[128,1024]{1,0:T(8,128)(2,1)} %reduce-scatter.4.cloned.1.call-done) | data formatting | bytes 524288
  437.2 6.1 %copy.49 = bf16[2,4,16,8,128]{4,3,2,1,0:T(8,128)(2,1)} copy(bf16[2,4,16,8,128]{3,2,1,0,4:T(8,128)(2,1)} %bitcast.558) | data formatting | bytes 524288
  (107 shorter events, 47.6 us)
Async XLA Ops:
  7.2 38.4 %copy-start = (bf16[128,16]{0,1:T(8,128)(2,1)S(1)}, bf16[128,16]{0,1:T(8,128)(2,1)}, u32[]{:S(2)}) copy-start(bf16[128,16]{0,1:T(8,128)(2,1)} %param.65) | copy-start | bytes 12292
  7.2 423.2 %reduce-scatter.4.cloned.1.call-start = ((), (), s32[]{:S(2)}) async-start(), calls=%async_computation.1 | async-start | bytes 786432
  8.2 24.4 %collective-permute-start = (bf16[2,2,16,8,128]{4,3,2,1,0:T(8,128)(2,1)S(1)}, bf16[2,2,16,8,128]{4,3,2,1,0:T(8,128)(2,1)S(1)}, u32[]{:S(2)}, u32[]{:S(2)}) collective-permute-start(bf16[2,2,16,8,128]{4,3,2,1,0:T(8,128)(2,1)S(1)} %slice.1486), channel_id=1, source_target_pairs={{0,2},{1,3},{4,6},{5,7},{8,10},{9,11},{12,14},{13,15},{16,18},{17,... | collective-permute-start | bytes 393224 | tf_op jit(solution)/shard_map/ppermute | solution.py:13
  35.0 2.3 copy-start.2
  45.6 2.2 copy-start.5
  55.7 1.8 copy-start.3
  229.8 31.2 %copy-start.6 = (bf16[1024,128]{1,0:T(8,128)(2,1)S(1)}, bf16[1024,128]{1,0:T(8,128)(2,1)}, u32[]{:S(2)}) copy-start(bf16[1024,128]{1,0:T(8,128)(2,1)} %copy-done.5) | copy-start | bytes 786436
  239.6 21.5 %collective-permute-start.1 = (f32[2,2,16,8,256]{4,3,2,1,0:T(8,128)S(1)}, f32[2,2,16,8,256]{4,3,2,1,0:T(8,128)S(1)}, u32[]{:S(2)}, u32[]{:S(2)}) collective-permute-start(f32[2,2,16,8,256]{4,3,2,1,0:T(8,128)S(1)} %slice.1599), channel_id=1, source_target_pairs={{2,0},{3,1},{6,4},{7,5},{10,8},{11,9},{14,12},{15,13},{18,16},{19,... | collective-permute-start | bytes 1572872 | tf_op jit(solution)/shard_map/ppermute | solution.py:13
  274.3 13.7 %copy-start.4 = (f32[27,256,128]{2,1,0:T(8,128)S(1)}, f32[27,256,128]{2,1,0:T(8,128)}, u32[]{:S(2)}) copy-start(f32[27,256,128]{2,1,0:T(8,128)} %copy-done.3) | copy-start | bytes 10616836
  288.0 155.3 %copy-start.1 = (bf16[128,16]{0,1:T(8,128)(2,1)S(1)}, bf16[128,16]{0,1:T(8,128)(2,1)}, u32[]{:S(2)}) copy-start(bf16[128,16]{0,1:T(8,128)(2,1)} %param.65) | copy-start | bytes 12292
Sparse Core Ops, SparseCore 0:
  288.1 10.2 reduce-scatter.3
where the time goes:
time: 454 us; the launch traced here: 450 us
  blocking collectives  177 us (39%)
  local copies, waits for them, and re-layouts  173 us (38%)
  matrix products  74.9 us (16%)
  between operations  14.6 us (3%)
  starting transfers between devices  6.18 us (1%)
    psum x1, blocking collectives, body(): lax.psum((grad_conv_local, grad_proj_local), ('cam', 'tm'))  142 us
    scatter-add x19, local copies, waits for them, and re-layouts, input_taps(): padded = padded.at[:, shift_t:shift_t + frames, shift_h:shift_h + height,...  125 us
    dot_general x27, matrix products, input_taps(): lax.dot_general(grad_rows, weight[tap_index], (((1,), (1,)), ((), ())), p...  55.4 us
    unnamed x20, local copies, waits for them, and re-layouts  40.4 us
    all_gather x1, blocking collectives, body(): block_in = lax.all_gather(cotangent, 'cam', axis=0, tiled=True)  13.6 us
    all_gather x1, blocking collectives, body(): block_in = lax.all_gather(latent_maps, 'cam', axis=0, tiled=True)  13.4 us
    dot_general x27, matrix products, weight_taps(): lax.dot_general(window, grad_rows, (((0,), (0,)), ((), ())), preferred_el...  9.49 us
  transfers between devices with their start and end apart: 3, of which 0 were waited for; matrix products, arithmetic and copies ran while one was open for 2% of the time, Pallas kernels for 0%

commit v1 on v0

--- a/solution.py
+++ b/solution.py
@@ -101,7 +101,19 @@
     cam_index = lax.axis_index("cam")
     my_row = lax.dynamic_slice_in_dim(mixing, cam_index, 1, 0)
     latent_maps = latent.reshape(cam_dev, frames, height, width * lat_width)
-    block_in = lax.all_gather(latent_maps, "cam", axis=0, tiled=True)
+    aux = lax.psum(1, "cam")
+    long_array = lax.axis_index("cam")
+    part_now, carry_out = (aux, long_array)
+    block_in, x_new = (latent_maps, 1)
+    while x_new < part_now:
+        table = []
+        for m in range(part_now):
+            table.append((m, m ^ x_new))
+        m_next = lax.ppermute(block_in, "cam", table)
+        v1 = jnp.concatenate([block_in, m_next], axis=0)
+        answer = jnp.concatenate([m_next, block_in], 0)
+        block_in = jnp.where(carry_out & x_new == 0, v1, answer)
+        x_new = 2 * x_new
     count_in = block_in.shape[0]
     flat_in = block_in.reshape(count_in, -1).astype(jnp.float32)
     added = jnp.dot(

time: 454 us -> 481 us (1.059); the launches traced: 450 us -> 472 us
  waiting for transfers between devices: 0.02 us -> 10.9 us
  matrix products: 74.9 us -> 82.7 us
    all_gather x1 -> x0, blocking collectives: 13.4 us -> none  [body(): block_in = lax.all_gather(latent_maps, 'cam', axis=0, tiled=True)]
    psum x1, blocking collectives: 142 us -> 152 us  [body(): lax.psum((grad_conv_local, grad_proj_local), ('cam', 'tm'))]
    unnamed x2, waiting for transfers between devices: 0.02 us -> 7.24 us
    unnamed x20 -> x111, local copies, waits for them, and re-layouts: 40.4 us -> 41.2 us
  transfers between devices with their start and end apart: 3 -> 5, of which waited for: 0 -> 2; matrix products, arithmetic and copies ran while one was open for 2% -> 44% of each run, Pallas kernels for 0% -> 0%
where the time goes in v1:
time: 481 us; the launch traced here: 472 us
  local copies, waits for them, and re-layouts  175 us (36%)
  blocking collectives  174 us (36%)
  matrix products  82.7 us (17%)
  between operations  15.5 us (3%)
  waiting for transfers between devices  10.9 us (2%)
  starting transfers between devices  9.4 us (2%)
    psum x1, blocking collectives, body(): lax.psum((grad_conv_local, grad_proj_local), ('cam', 'tm'))  152 us
    scatter-add x19, local copies, waits for them, and re-layouts, input_taps(): padded = padded.at[:, shift_t:shift_t + frames, shift_h:shift_h + height,...  126 us
    dot_general x27, matrix products, input_taps(): lax.dot_general(grad_rows, weight[tap_index], (((1,), (1,)), ((), ())), p...  56.2 us
    unnamed x111, local copies, waits for them, and re-layouts  41.2 us
    all_gather x1, blocking collectives, body(): block_in = lax.all_gather(cotangent, 'cam', axis=0, tiled=True)  13.6 us
    dot_general x27, matrix products, weight_taps(): lax.dot_general(window, grad_rows, (((0,), (0,)), ((), ())), preferred_el...  13.5 us
  transfers between devices with their start and end apart: 5, of which 2 were waited for; matrix products, arithmetic and copies ran while one was open for 44% of the time, Pallas kernels for 0%

profile of v1, /device:TPU:0, one launch (start us, length us, event | category | flops | bytes accessed | tf_op | source)
XLA Modules:
  0.0 471.6 jit_solution(12707462941861025695)
XLA Ops:
  8.2 4.8 %collective-permute-start = (bf16[2,2,16,8,128]{4,3,2,1,0:T(8,128)(2,1)S(1)}, bf16[2,2,16,8,128]{4,3,2,1,0:T(8,128)(2,1)S(1)}, u32[]{:S(2)}, u32[]{:S(2)}) collective-permute-start(bf16[2,2,16,8,128]{4,3,2,1,0:T(8,128)(2,1)S(1)} %slice.1486), channel_id=1, source_target_pairs={{0,2},{1,3},{4,6},{5,7},{8,10},{9,11},{12,14},{13,15},{16,18},{17,... | collective-permute-start | bytes 393224 | tf_op jit(solution)/shard_map/ppermute | solution.py:13
  15.4 13.6 %all_gather.11 = bf16[4,4,16,128]{3,2,1,0:T(8,128)(2,1)S(1)} all-gather(bf16[1,4,16,128]{3,2,1,0:T(8,128)(2,1)} %param.69), channel_id=1, replica_groups=mesh['groups'=2,'cam'=4,'tm'=2,'chan'=2] {'cam'}, dimensions={0}, use_global_device_ids=true | all-gather | bytes 81920 | tf_op jit(solution)/shard_map/all_gather | solution.py:126
  30.2 2.4 all_gather.10
  32.6 2.0 all_gather.9
  35.1 2.1 pad_slice_fusion
  47.7 4.1 psum.21
  73.8 2.3 scatter-add.94
  76.1 7.2 %scatter-add.95 = f32[2,6,18,10,256]{4,3,2,1,0:T(8,128)} dynamic-update-slice(f32[2,6,18,10,256]{4,3,2,1,0:T(8,128)} %scatter-add.94, f32[2,4,16,8,256]{4,3,2,1,0:T(8,128)} %convolution_add_fusion.25, s32[]{:T(128)} %constant.918.clone.1, s32[]{:T(128)} %constant.918.clone.1, s32[]{:T(128)} %constant.918.clone.1, s32[]{:T(128)} %constant.925.clone.1, s32[]{:T(128)} %constant.918.clone.1) | dynamic-update-slice | bytes 2097156 | tf_op jit(solution)/shard_map/scatter-add | solution.py:66
  85.2 6.7 %scatter-add.96 = f32[2,6,18,10,256]{4,3,2,1,0:T(8,128)} dynamic-update-slice(f32[2,6,18,10,256]{4,3,2,1,0:T(8,128)} %scatter-add.95, f32[2,4,16,8,256]{4,3,2,1,0:T(8,128)S(1)} %convolution_add_fusion.24, s32[]{:T(128)} %constant.918.clone.1, s32[]{:T(128)} %constant.918.clone.1, s32[]{:T(128)} %constant.918.clone.1, s32[]{:T(128)} %constant.924.clone.1, s32[]{:T(128)} %constant.918.clone.1) | dynamic-update-slice | bytes 2097156 | tf_op jit(solution)/shard_map/scatter-add | solution.py:66
  91.9 2.6 fusion.7
  96.3 6.7 %scatter-add.100 = f32[2,6,18,10,256]{4,3,2,1,0:T(8,128)} dynamic-update-slice(f32[2,6,18,10,256]{4,3,2,1,0:T(8,128)} %fusion.7, f32[2,4,16,8,256]{4,3,2,1,0:T(8,128)S(1)} %convolution_add_fusion.22, s32[]{:T(128)} %constant.918.clone.1, s32[]{:T(128)} %constant.918.clone.1, s32[]{:T(128)} %constant.925.clone.1, s32[]{:T(128)} %constant.925.clone.1, s32[]{:T(128)} %constant.918.clone.1) | dynamic-update-slice | bytes 2097156 | tf_op jit(solution)/shard_map/scatter-add | solution.py:66
  103.1 3.8 convolution_add_fusion.21
  106.9 8.7 %scatter-add.101 = f32[2,6,18,10,256]{4,3,2,1,0:T(8,128)} dynamic-update-slice(f32[2,6,18,10,256]{4,3,2,1,0:T(8,128)} %scatter-add.100, f32[2,4,16,8,256]{4,3,2,1,0:T(8,128)S(1)} %convolution_add_fusion.21, s32[]{:T(128)} %constant.918.clone.1, s32[]{:T(128)} %bitcast.103, s32[]{:T(128)} %bitcast.104, s32[]{:T(128)} %bitcast.105, s32[]{:T(128)} %constant.918.clone.1) | dynamic-update-slice | bytes 2097156 | tf_op jit(solution)/shard_map/scatter-add | solution.py:66
  115.5 2.6 fusion.6
  118.1 1.9 convolution_add_fusion.19
  120.0 6.7 %scatter-add.105 = f32[2,6,18,10,256]{4,3,2,1,0:T(8,128)} dynamic-update-slice(f32[2,6,18,10,256]{4,3,2,1,0:T(8,128)} %fusion.6, f32[2,4,16,8,256]{4,3,2,1,0:T(8,128)S(1)} %convolution_add_fusion.19, s32[]{:T(128)} %constant.918.clone.1, s32[]{:T(128)} %constant.918.clone.1, s32[]{:T(128)} %constant.924.clone.1, s32[]{:T(128)} %constant.925.clone.1, s32[]{:T(128)} %constant.918.clone.1) | dynamic-update-slice | bytes 2097156 | tf_op jit(solution)/shard_map/scatter-add | solution.py:66
  126.7 1.9 convolution_add_fusion.18
  128.6 6.7 %scatter-add.106 = f32[2,6,18,10,256]{4,3,2,1,0:T(8,128)} dynamic-update-slice(f32[2,6,18,10,256]{4,3,2,1,0:T(8,128)} %scatter-add.105, f32[2,4,16,8,256]{4,3,2,1,0:T(8,128)S(1)} %convolution_add_fusion.18, s32[]{:T(128)} %constant.918.clone.1, s32[]{:T(128)} %constant.918.clone.1, s32[]{:T(128)} %constant.924.clone.1, s32[]{:T(128)} %constant.924.clone.1, s32[]{:T(128)} %constant.918.clone.1) | dynamic-update-slice | bytes 2097156 | tf_op jit(solution)/shard_map/scatter-add | solution.py:66
  135.3 2.6 fusion.5
  138.0 1.9 convolution_add_fusion.16
  139.9 6.7 %scatter-add.110 = f32[2,6,18,10,256]{4,3,2,1,0:T(8,128)} dynamic-update-slice(f32[2,6,18,10,256]{4,3,2,1,0:T(8,128)} %fusion.5, f32[2,4,16,8,256]{4,3,2,1,0:T(8,128)S(1)} %convolution_add_fusion.16, s32[]{:T(128)} %constant.918.clone.1, s32[]{:T(128)} %constant.925.clone.1, s32[]{:T(128)} %constant.918.clone.1, s32[]{:T(128)} %constant.925.clone.1, s32[]{:T(128)} %constant.918.clone.1) | dynamic-update-slice | bytes 2097156 | tf_op jit(solution)/shard_map/scatter-add | solution.py:66
  146.6 1.9 convolution_add_fusion.15
  148.5 6.7 %scatter-add.111 = f32[2,6,18,10,256]{4,3,2,1,0:T(8,128)} dynamic-update-slice(f32[2,6,18,10,256]{4,3,2,1,0:T(8,128)} %scatter-add.110, f32[2,4,16,8,256]{4,3,2,1,0:T(8,128)S(1)} %convolution_add_fusion.15, s32[]{:T(128)} %constant.918.clone.1, s32[]{:T(128)} %constant.925.clone.1, s32[]{:T(128)} %constant.918.clone.1, s32[]{:T(128)} %constant.924.clone.1, s32[]{:T(128)} %constant.918.clone.1) | dynamic-update-slice | bytes 2097156 | tf_op jit(solution)/shard_map/scatter-add | solution.py:66
  155.3 2.6 fusion.4
  157.9 1.9 convolution_add_fusion.13
  159.8 6.7 %scatter-add.115 = f32[2,6,18,10,256]{4,3,2,1,0:T(8,128)} dynamic-update-slice(f32[2,6,18,10,256]{4,3,2,1,0:T(8,128)} %fusion.4, f32[2,4,16,8,256]{4,3,2,1,0:T(8,128)S(1)} %convolution_add_fusion.13, s32[]{:T(128)} %constant.918.clone.1, s32[]{:T(128)} %constant.925.clone.1, s32[]{:T(128)} %constant.925.clone.1, s32[]{:T(128)} %constant.925.clone.1, s32[]{:T(128)} %constant.918.clone.1) | dynamic-update-slice | bytes 2097156 | tf_op jit(solution)/shard_map/scatter-add | solution.py:66
  168.4 6.7 %scatter-add.116 = f32[2,6,18,10,256]{4,3,2,1,0:T(8,128)} dynamic-update-slice(f32[2,6,18,10,256]{4,3,2,1,0:T(8,128)} %scatter-add.115, f32[2,4,16,8,256]{4,3,2,1,0:T(8,128)S(1)} %convolution_add_fusion.12, s32[]{:T(128)} %constant.918.clone.1, s32[]{:T(128)} %constant.925.clone.1, s32[]{:T(128)} %constant.925.clone.1, s32[]{:T(128)} %constant.924.clone.1, s32[]{:T(128)} %constant.918.clone.1) | dynamic-update-slice | bytes 2097156 | tf_op jit(solution)/shard_map/scatter-add | solution.py:66
  175.1 2.6 fusion.3
  179.6 6.7 %scatter-add.120 = f32[2,6,18,10,256]{4,3,2,1,0:T(8,128)} dynamic-update-slice(f32[2,6,18,10,256]{4,3,2,1,0:T(8,128)} %fusion.3, f32[2,4,16,8,256]{4,3,2,1,0:T(8,128)S(1)} %convolution_add_fusion.10, s32[]{:T(128)} %constant.918.clone.1, s32[]{:T(128)} %constant.925.clone.1, s32[]{:T(128)} %constant.924.clone.1, s32[]{:T(128)} %constant.925.clone.1, s32[]{:T(128)} %constant.918.clone.1) | dynamic-update-slice | bytes 2097156 | tf_op jit(solution)/shard_map/scatter-add | solution.py:66
  188.2 6.7 %scatter-add.121 = f32[2,6,18,10,256]{4,3,2,1,0:T(8,128)} dynamic-update-slice(f32[2,6,18,10,256]{4,3,2,1,0:T(8,128)} %scatter-add.120, f32[2,4,16,8,256]{4,3,2,1,0:T(8,128)S(1)} %convolution_add_fusion.9, s32[]{:T(128)} %constant.918.clone.1, s32[]{:T(128)} %constant.925.clone.1, s32[]{:T(128)} %constant.924.clone.1, s32[]{:T(128)} %constant.924.clone.1, s32[]{:T(128)} %constant.918.clone.1) | dynamic-update-slice | bytes 2097156 | tf_op jit(solution)/shard_map/scatter-add | solution.py:66
  194.9 2.6 fusion.2
  197.5 1.9 convolution_add_fusion.7
  199.4 6.7 %scatter-add.125 = f32[2,6,18,10,256]{4,3,2,1,0:T(8,128)} dynamic-update-slice(f32[2,6,18,10,256]{4,3,2,1,0:T(8,128)} %fusion.2, f32[2,4,16,8,256]{4,3,2,1,0:T(8,128)S(1)} %convolution_add_fusion.7, s32[]{:T(128)} %constant.918.clone.1, s32[]{:T(128)} %constant.924.clone.1, s32[]{:T(128)} %constant.918.clone.1, s32[]{:T(128)} %constant.925.clone.1, s32[]{:T(128)} %constant.918.clone.1) | dynamic-update-slice | bytes 2097156 | tf_op jit(solution)/shard_map/scatter-add | solution.py:66
  208.0 6.7 %scatter-add.126 = f32[2,6,18,10,256]{4,3,2,1,0:T(8,128)} dynamic-update-slice(f32[2,6,18,10,256]{4,3,2,1,0:T(8,128)} %scatter-add.125, f32[2,4,16,8,256]{4,3,2,1,0:T(8,128)S(1)} %convolution_add_fusion.6, s32[]{:T(128)} %constant.918.clone.1, s32[]{:T(128)} %constant.924.clone.1, s32[]{:T(128)} %constant.918.clone.1, s32[]{:T(128)} %constant.924.clone.1, s32[]{:T(128)} %constant.918.clone.1) | dynamic-update-slice | bytes 2097156 | tf_op jit(solution)/shard_map/scatter-add | solution.py:66
  214.8 2.6 fusion.1
  219.2 6.7 %scatter-add.130 = f32[2,6,18,10,256]{4,3,2,1,0:T(8,128)} dynamic-update-slice(f32[2,6,18,10,256]{4,3,2,1,0:T(8,128)} %fusion.1, f32[2,4,16,8,256]{4,3,2,1,0:T(8,128)S(1)} %convolution_add_fusion.4, s32[]{:T(128)} %constant.918.clone.1, s32[]{:T(128)} %constant.924.clone.1, s32[]{:T(128)} %constant.925.clone.1, s32[]{:T(128)} %constant.925.clone.1, s32[]{:T(128)} %constant.918.clone.1) | dynamic-update-slice | bytes 2097156 | tf_op jit(solution)/shard_map/scatter-add | solution.py:66
  227.8 6.7 %scatter-add.131 = f32[2,6,18,10,256]{4,3,2,1,0:T(8,128)} dynamic-update-slice(f32[2,6,18,10,256]{4,3,2,1,0:T(8,128)} %scatter-add.130, f32[2,4,16,8,256]{4,3,2,1,0:T(8,128)S(1)} %convolution_add_fusion.3, s32[]{:T(128)} %constant.918.clone.1, s32[]{:T(128)} %constant.924.clone.1, s32[]{:T(128)} %constant.925.clone.1, s32[]{:T(128)} %constant.924.clone.1, s32[]{:T(128)} %constant.918.clone.1) | dynamic-update-slice | bytes 2097156 | tf_op jit(solution)/shard_map/scatter-add | solution.py:66
  234.5 2.6 fusion
  239.0 6.7 %scatter-add.135 = f32[2,6,18,10,256]{4,3,2,1,0:T(8,128)} dynamic-update-slice(f32[2,6,18,10,256]{4,3,2,1,0:T(8,128)} %fusion, f32[2,4,16,8,256]{4,3,2,1,0:T(8,128)S(1)} %convolution_add_fusion.1, s32[]{:T(128)} %constant.918.clone.1, s32[]{:T(128)} %constant.924.clone.1, s32[]{:T(128)} %constant.924.clone.1, s32[]{:T(128)} %constant.925.clone.1, s32[]{:T(128)} %constant.918.clone.1) | dynamic-update-slice | bytes 2097156 | tf_op jit(solution)/shard_map/scatter-add | solution.py:66
  245.7 1.9 convolution_add_fusion
  247.6 6.9 %scatter-add.136 = f32[2,6,18,10,256]{4,3,2,1,0:T(8,128)} dynamic-update-slice(f32[2,6,18,10,256]{4,3,2,1,0:T(8,128)} %scatter-add.135, f32[2,4,16,8,256]{4,3,2,1,0:T(8,128)S(1)} %convolution_add_fusion, s32[]{:T(128)} %constant.918.clone.1, s32[]{:T(128)} %constant.924.clone.1, s32[]{:T(128)} %constant.924.clone.1, s32[]{:T(128)} %constant.924.clone.1, s32[]{:T(128)} %constant.918.clone.1) | dynamic-update-slice | bytes 2097156 | tf_op jit(solution)/shard_map/scatter-add | solution.py:66
  257.1 152.1 %all-reduce.4 = (bf16[27,256,128]{2,1,0:T(8,128)(2,1)}, f32[128,16]{0,1:T(8,128)}) all-reduce(f32[27,256,128]{2,1,0:T(8,128)} %copy-done.47, f32[128,16]{0,1:T(8,128)S(1)} %fusion.156), channel_id=1, replica_groups=mesh['groups'=2,'cam'=4,'tm'=2,'chan'=2] {'cam','tm'}, use_global_device_ids=true, to_apply=%region_5.6 | all-reduce | flops 886784 | bytes 5324800 | tf_op jit(solution)/shard_map/psum | solution.py:150
  412.9 3.7 collective-permute-done.2
  418.0 11.8 %copy.51 = bf16[2,4,16,8,256]{3,2,1,0,4:T(8,128)(2,1)} copy(bf16[2,4,16,8,256]{4,3,2,1,0:T(8,128)(2,1)S(1)} %fusion.37) | data formatting | bytes 1048576
  429.8 13.5 %reshape.1534 = bf16[256,1024]{1,0:T(8,128)(2,1)} reshape(bf16[256,2,4,16,8]{4,3,2,1,0:T(8,128)(2,1)} %bitcast.562) | data formatting | bytes 1048576
  444.3 7.2 %reduce-scatter.4.cloned.1.call-done = bf16[128,1024]{1,0:T(8,128)(2,1)} async-done(((bf16[256,1024]{1,0:T(8,128)(2,1)}), bf16[128,1024]{1,0:T(8,128)(2,1)}) %reduce-scatter.4.cloned.1.call-update) | async-done | bytes 262160
  451.5 6.8 %reshape.1535 = bf16[128,2,4,16,8]{4,3,2,1,0:T(8,128)(2,1)} reshape(bf16[128,1024]{1,0:T(8,128)(2,1)} %reduce-scatter.4.cloned.1.call-done) | data formatting | bytes 524288
  458.4 6.1 %copy.52 = bf16[2,4,16,8,128]{4,3,2,1,0:T(8,128)(2,1)} copy(bf16[2,4,16,8,128]{3,2,1,0,4:T(8,128)(2,1)} %bitcast.563) | data formatting | bytes 524288
  (205 shorter events, 62.1 us)
Async XLA Ops:
  7.2 40.3 %copy-start = (bf16[128,16]{0,1:T(8,128)(2,1)S(1)}, bf16[128,16]{0,1:T(8,128)(2,1)}, u32[]{:S(2)}) copy-start(bf16[128,16]{0,1:T(8,128)(2,1)} %param.65) | copy-start | bytes 12292
  7.2 444.4 %reduce-scatter.4.cloned.1.call-start = ((), (), s32[]{:S(2)}) async-start(), calls=%async_computation.1 | async-start | bytes 786432
  8.2 24.4 %collective-permute-start = (bf16[2,2,16,8,128]{4,3,2,1,0:T(8,128)(2,1)S(1)}, bf16[2,2,16,8,128]{4,3,2,1,0:T(8,128)(2,1)S(1)}, u32[]{:S(2)}, u32[]{:S(2)}) collective-permute-start(bf16[2,2,16,8,128]{4,3,2,1,0:T(8,128)(2,1)S(1)} %slice.1486), channel_id=1, source_target_pairs={{0,2},{1,3},{4,6},{5,7},{8,10},{9,11},{12,14},{13,15},{16,18},{17,... | collective-permute-start | bytes 393224 | tf_op jit(solution)/shard_map/ppermute | solution.py:13
  29.6 24.2 %copy-start.50 = (bf16[1024,16]{1,0:T(8,128)(2,1)}, bf16[1024,16]{1,0:T(8,128)(2,1)S(1)}, u32[]{:S(2)}) copy-start(bf16[1024,16]{1,0:T(8,128)(2,1)S(1)} %reshape.1501) | copy-start | bytes 98308
  35.1 3.8 copy-start.11
  35.1 6.6 %copy-start.9 = (bf16[2,4,16,8,256]{4,3,2,1,0:T(8,128)(2,1)}, bf16[2,4,16,8,256]{4,3,2,1,0:T(8,128)(2,1)S(1)}, u32[]{:S(2)}) copy-start(bf16[2,4,16,8,256]{4,3,2,1,0:T(8,128)(2,1)S(1)} %get-tuple-element.367) | copy-start | bytes 1572868
  35.1 9.1 %copy-start.7 = (bf16[2,4,16,8,256]{4,3,2,1,0:T(8,128)(2,1)}, bf16[2,4,16,8,256]{4,3,2,1,0:T(8,128)(2,1)S(1)}, u32[]{:S(2)}) copy-start(bf16[2,4,16,8,256]{4,3,2,1,0:T(8,128)(2,1)S(1)} %get-tuple-element.364) | copy-start | bytes 1572868
  35.1 9.7 %copy-start.5 = (bf16[2,4,16,8,256]{4,3,2,1,0:T(8,128)(2,1)}, bf16[2,4,16,8,256]{4,3,2,1,0:T(8,128)(2,1)S(1)}, u32[]{:S(2)}) copy-start(bf16[2,4,16,8,256]{4,3,2,1,0:T(8,128)(2,1)S(1)} %get-tuple-element.365) | copy-start | bytes 1572868
  35.1 10.0 %copy-start.3 = (bf16[2,4,16,8,256]{4,3,2,1,0:T(8,128)(2,1)}, bf16[2,4,16,8,256]{4,3,2,1,0:T(8,128)(2,1)S(1)}, u32[]{:S(2)}) copy-start(bf16[2,4,16,8,256]{4,3,2,1,0:T(8,128)(2,1)S(1)} %get-tuple-element.366) | copy-start | bytes 1572868
  37.3 2.8 copy-start.36
  37.3 3.1 copy-start.34
  37.3 3.4 copy-start.32
  37.3 3.7 copy-start.30
  37.3 4.0 copy-start.28
  37.3 4.6 copy-start.42
  37.3 4.6 copy-start.44
  37.3 4.6 copy-start.45
  37.3 4.6 copy-start.46
  37.3 4.6 copy-start.26
  37.4 4.9 %copy-start.24 = (bf16[2,4,16,8,256]{4,3,2,1,0:T(8,128)(2,1)}, bf16[2,4,16,8,256]{4,3,2,1,0:T(8,128)(2,1)S(1)}, u32[]{:S(2)}) copy-start(bf16[2,4,16,8,256]{4,3,2,1,0:T(8,128)(2,1)S(1)} %get-tuple-element.357) | copy-start | bytes 1572868
  37.4 5.2 %copy-start.22 = (bf16[2,4,16,8,256]{4,3,2,1,0:T(8,128)(2,1)}, bf16[2,4,16,8,256]{4,3,2,1,0:T(8,128)(2,1)S(1)}, u32[]{:S(2)}) copy-start(bf16[2,4,16,8,256]{4,3,2,1,0:T(8,128)(2,1)S(1)} %get-tuple-element.358) | copy-start | bytes 1572868
  37.4 5.5 %copy-start.20 = (bf16[2,4,16,8,256]{4,3,2,1,0:T(8,128)(2,1)}, bf16[2,4,16,8,256]{4,3,2,1,0:T(8,128)(2,1)S(1)}, u32[]{:S(2)}) copy-start(bf16[2,4,16,8,256]{4,3,2,1,0:T(8,128)(2,1)S(1)} %get-tuple-element.359) | copy-start | bytes 1572868
  37.4 5.8 %copy-start.18 = (bf16[2,4,16,8,256]{4,3,2,1,0:T(8,128)(2,1)}, bf16[2,4,16,8,256]{4,3,2,1,0:T(8,128)(2,1)S(1)}, u32[]{:S(2)}) copy-start(bf16[2,4,16,8,256]{4,3,2,1,0:T(8,128)(2,1)S(1)} %get-tuple-element.360) | copy-start | bytes 1572868
  37.4 6.2 %copy-start.16 = (bf16[2,4,16,8,256]{4,3,2,1,0:T(8,128)(2,1)}, bf16[2,4,16,8,256]{4,3,2,1,0:T(8,128)(2,1)S(1)}, u32[]{:S(2)}) copy-start(bf16[2,4,16,8,256]{4,3,2,1,0:T(8,128)(2,1)S(1)} %get-tuple-element.361) | copy-start | bytes 1572868
  37.4 6.5 %copy-start.14 = (bf16[2,4,16,8,256]{4,3,2,1,0:T(8,128)(2,1)}, bf16[2,4,16,8,256]{4,3,2,1,0:T(8,128)(2,1)S(1)}, u32[]{:S(2)}) copy-start(bf16[2,4,16,8,256]{4,3,2,1,0:T(8,128)(2,1)S(1)} %get-tuple-element.362) | copy-start | bytes 1572868
  37.4 8.3 %copy-start.48 = (bf16[2,4,16,8,256]{4,3,2,1,0:T(8,128)(2,1)}, bf16[2,4,16,8,256]{4,3,2,1,0:T(8,128)(2,1)S(1)}, u32[]{:S(2)}) copy-start(bf16[2,4,16,8,256]{4,3,2,1,0:T(8,128)(2,1)S(1)} %get-tuple-element.344) | copy-start | bytes 1572868
  52.1 10.2 %copy-start.12 = (bf16[2,4,16,8,256]{4,3,2,1,0:T(8,128)(2,1)S(1)}, bf16[2,4,16,8,256]{4,3,2,1,0:T(8,128)(2,1)}, u32[]{:S(2)}) copy-start(bf16[2,4,16,8,256]{4,3,2,1,0:T(8,128)(2,1)} %copy-done.11) | copy-start | bytes 1572868
  52.2 358.9 %collective-permute-start.1 = (bf16[2,4,16,128]{3,2,1,0:T(8,128)(2,1)S(1)}, bf16[2,4,16,128]{3,2,1,0:T(8,128)(2,1)S(1)}, u32[]{:S(2)}, u32[]{:S(2)}) collective-permute-start(bf16[2,4,16,128]{3,2,1,0:T(8,128)(2,1)S(1)} %reshape.1498), channel_id=1, source_target_pairs={{0,4},{4,0},{8,12},{12,8},{1,5},{5,1},{9,13},{13,9},{2,6},{6,2},{1... | collective-permute-start | bytes 98312 | tf_op jit(solution)/shard_map/ppermute | solution.py:112
  55.0 7.7 %copy-start.43 = (bf16[2,4,16,8,256]{4,3,2,1,0:T(8,128)(2,1)S(1)}, bf16[2,4,16,8,256]{4,3,2,1,0:T(8,128)(2,1)}, u32[]{:S(2)}) copy-start(bf16[2,4,16,8,256]{4,3,2,1,0:T(8,128)(2,1)} %copy-done.42) | copy-start | bytes 1572868
  55.0 8.1 %copy-start.41 = (bf16[2,4,16,8,256]{4,3,2,1,0:T(8,128)(2,1)S(1)}, bf16[2,4,16,8,256]{4,3,2,1,0:T(8,128)(2,1)}, u32[]{:S(2)}) copy-start(bf16[2,4,16,8,256]{4,3,2,1,0:T(8,128)(2,1)} %copy-done.40) | copy-start | bytes 1572868
  56.5 7.0 %copy-start.39 = (bf16[2,4,16,8,256]{4,3,2,1,0:T(8,128)(2,1)S(1)}, bf16[2,4,16,8,256]{4,3,2,1,0:T(8,128)(2,1)}, u32[]{:S(2)}) copy-start(bf16[2,4,16,8,256]{4,3,2,1,0:T(8,128)(2,1)} %copy-done.38) | copy-start | bytes 1572868
  56.5 7.3 %copy-start.37 = (bf16[2,4,16,8,256]{4,3,2,1,0:T(8,128)(2,1)S(1)}, bf16[2,4,16,8,256]{4,3,2,1,0:T(8,128)(2,1)}, u32[]{:S(2)}) copy-start(bf16[2,4,16,8,256]{4,3,2,1,0:T(8,128)(2,1)} %copy-done.36) | copy-start | bytes 1572868
  58.0 6.2 %copy-start.35 = (bf16[2,4,16,8,256]{4,3,2,1,0:T(8,128)(2,1)S(1)}, bf16[2,4,16,8,256]{4,3,2,1,0:T(8,128)(2,1)}, u32[]{:S(2)}) copy-start(bf16[2,4,16,8,256]{4,3,2,1,0:T(8,128)(2,1)} %copy-done.34) | copy-start | bytes 1572868
  59.4 5.1 %copy-start.33 = (bf16[2,4,16,8,256]{4,3,2,1,0:T(8,128)(2,1)S(1)}, bf16[2,4,16,8,256]{4,3,2,1,0:T(8,128)(2,1)}, u32[]{:S(2)}) copy-start(bf16[2,4,16,8,256]{4,3,2,1,0:T(8,128)(2,1)} %copy-done.32) | copy-start | bytes 1572868
  60.9 4.0 copy-start.31
  62.3 2.9 copy-start.29
  62.7 2.9 copy-start.10
  63.1 2.9 copy-start.27
  63.4 2.9 copy-start.25
  63.8 2.9 copy-start.23
  64.1 2.9 copy-start.21
  64.5 2.8 copy-start.19
  64.9 2.8 copy-start.17
  65.2 2.8 copy-start.15
  65.6 2.8 copy-start.8
  255.8 160.8 %collective-permute-start.3 = (f32[2,2,16,8,256]{4,3,2,1,0:T(8,128)S(1)}, f32[2,2,16,8,256]{4,3,2,1,0:T(8,128)S(1)}, u32[]{:S(2)}, u32[]{:S(2)}) collective-permute-start(f32[2,2,16,8,256]{4,3,2,1,0:T(8,128)S(1)} %slice.1599), channel_id=1, source_target_pairs={{2,0},{3,1},{6,4},{7,5},{10,8},{11,9},{14,12},{15,13},{18,16},{19,... | collective-permute-start | bytes 1572872 | tf_op jit(solution)/shard_map/ppermute | solution.py:13
  411.1 5.4 %collective-permute-start.2 = (bf16[4,4,16,128]{3,2,1,0:T(8,128)(2,1)S(1)}, bf16[4,4,16,128]{3,2,1,0:T(8,128)(2,1)S(1)}, u32[]{:S(2)}, u32[]{:S(2)}) collective-permute-start(bf16[4,4,16,128]{3,2,1,0:T(8,128)(2,1)S(1)} %maximum_select_fusion.2), channel_id=1, source_target_pairs={{0,8},{4,12},{8,0},{12,4},{1,9},{5,13},{9,1},{13,5},{2,10},{6,14},... | collective-permute-start | bytes 196616 | tf_op jit(solution)/shard_map/ppermute | solution.py:112
  443.4 21.1 %copy-start.1 = (bf16[128,16]{0,1:T(8,128)(2,1)S(1)}, bf16[128,16]{0,1:T(8,128)(2,1)}, u32[]{:S(2)}) copy-start(bf16[128,16]{0,1:T(8,128)(2,1)} %param.65) | copy-start | bytes 12292
  (9 other events, 20.6 us)
Sparse Core Ops, SparseCore 0:
  443.4 8.0 reduce-scatter.3
